TPU v7x, 32 devices: a whole 2x2x4 slice. The times are simulated.
32 devices in a mesh: row: 2 (over x), col: 4 (over z), tok: 4 (over y, core).
Axes of the slice: x: 2, y: 2, z: 4, core: 2. Of those that a mesh axis runs over, the one named last changes fastest.
Arguments:
- activations: bfloat16 [4096, 2048], P(('row', 'col', 'tok')), may hold values from -6 to 6
- norm_gain: float32 [2048], replicated, may hold values from 0.1 to 1.9
- routes: int32 [4096, 8], P(('row', 'col', 'tok')), may hold values from 0 to 127, all different within a row; in each aligned block of 128 rows (0 to 127, 128 to 255, ...) at most 10 rows name the same one
- route_weights: float32 [4096, 8], P(('row', 'col', 'tok')), may hold values from 0.05 to 1
- gate_up_weight: bfloat16 [128, 2, 768, 2048], P(('row', 'col'), None, 'tok'), may hold values from -0.125 to 0.125
- down_weight: bfloat16 [128, 768, 2048], P(('row', 'col'), 'tok'), may hold values from -0.21875 to 0.21875
Outputs:
- expert_mix: bfloat16 [4096, 2048], P(('row', 'col', 'tok'))
Inputs may be any that keep to these rules, and one draw needn't show every extreme that they name: `routes`: within the rows of one device no expert is named by more than 10 rows, a bound that some block reaches.
All inputs are finite; a program needn't handle non-finite values.
Results may differ from a plain program's by a relative error of at most 0.0085.
Values may be sent and summed in bfloat16 or wider, within the bound.
No kernel may reach another device: no remote copies, remote signals or barrier semaphores. Data moves between devices by JAX's collectives and lax.ppermute only.
A program may use at most 384 MiB of HBM per device.

v0:
```python
import jax
import jax.numpy as jnp
from jax import lax
from jax.sharding import PartitionSpec as P

CAP = 10
EPSILON = 1e-06


def rank_in_block(block_routes, experts):
    onehot = (block_routes[:, None] == jnp.arange(experts, dtype=jnp.int32)[None, :]).astype(
        jnp.int32
    )
    before = jnp.cumsum(onehot, axis=0) - onehot
    return jnp.sum(before * onehot, axis=1)


def rms_normed(activations, norm_gain):
    values = activations.astype(jnp.float32)
    scale = lax.rsqrt(jnp.mean(values * values, axis=-1, keepdims=True) + EPSILON)
    return (values * scale * norm_gain).astype(jnp.bfloat16)


def apply_experts(received, gate_up_weight, down_weight):
    both = jnp.einsum(
        "sjcd,jgfd->sjcgf",
        received,
        lax.all_gather(gate_up_weight, "tok", axis=2, tiled=True),
        preferred_element_type=jnp.float32,
    )
    hidden = (jax.nn.silu(both[:, :, :, 0, :]) * both[:, :, :, 1, :]).astype(jnp.bfloat16)
    summed = jnp.einsum(
        "sjcf,jfd->sjcd",
        hidden,
        lax.all_gather(down_weight, "tok", axis=1, tiled=True),
        preferred_element_type=jnp.float32,
    )
    return summed.astype(jnp.bfloat16)


def local(activations, norm_gain, routes, route_weights, gate_up_weight, down_weight):
    count, features = activations.shape
    chosen = routes.shape[1]
    holding = gate_up_weight.shape[0]
    row_count = lax.axis_size("row")
    col_count = lax.axis_size("col")
    owners = row_count * col_count
    experts = holding * owners
    normed = rms_normed(activations, norm_gain)
    gates = route_weights / jnp.sum(route_weights, axis=1, keepdims=True)
    flat_routes = routes.reshape(-1)
    target = flat_routes * CAP + rank_in_block(flat_routes, experts)
    token_ids = jnp.arange(count * chosen, dtype=jnp.int32) // chosen
    source = jnp.full((experts * CAP,), count, jnp.int32).at[target].set(token_ids)
    outbound = jnp.take(normed, source, axis=0, mode="fill", fill_value=0)
    outbound = outbound.reshape(owners, holding, CAP, features)
    arrived = lax.all_to_all(outbound, ("row", "col"), split_axis=0, concat_axis=0, tiled=True)
    results = apply_experts(arrived, gate_up_weight, down_weight)
    returned = lax.all_to_all(results, ("row", "col"), split_axis=0, concat_axis=0, tiled=True)
    picked = jnp.take(returned.reshape(experts * CAP, features), target, axis=0)
    picked = picked.reshape(count, chosen, features)
    mixed = jnp.einsum("tk,tkd->td", gates, picked.astype(jnp.float32))
    return mixed.astype(jnp.bfloat16)


def solution(mesh):
    in_specs = (
        P(("row", "col", "tok"), None),
        P(),
        P(("row", "col", "tok"), None),
        P(("row", "col", "tok"), None),
        P(("row", "col"), None, "tok", None),
        P(("row", "col"), "tok", None),
    )
    out_specs = P(("row", "col", "tok"), None)
    return jax.shard_map(local, mesh=mesh, in_specs=in_specs, out_specs=out_specs, check_vma=False)
```

profile of v0, /device:TPU:0, one launch (start us, length us, event | category | flops | bytes accessed | tf_op | source)
XLA Modules:
  0.0 1096.7 jit_solution(4971576280621673986)
XLA Ops:
  6.5 0.7 all-gather.3.cloned.1.call-update
  7.3 0.7 all-gather.5.cloned.1.call-update
  8.4 0.2 fusion.24
  9.1 0.4 fusion.23
  9.5 0.6 copy-done.1
  10.0 4.3 scatter_custom_fusion
  14.6 0.2 fusion.21
  14.8 6.2 gather_fusion
  21.0 10.5 gather.13
  31.8 12.9 %broadcast_select_fusion = bf16[8,16,10,2048]{3,2,1,0:T(8,128)(2,1)} fusion(bf16[8,16,10,2048]{3,2,1,0:T(8,128)(2,1)} %gather.13, pred[8,16,10]{2,1,0:T(8,128)(4,1)S(1)} %broadcast_in_dim.34), kind=kLoop, calls=%fused_computation.9 | loop fusion | flops 2621440 | bytes 10487040 | tf_op jit(solution)/shard_map/jit(_take)/select_n | solution.py:55
  44.6 8.0 copy.35
  52.6 123.2 %all_to_all.10 = bf16[8,16,10,2048]{3,1,2,0:T(8,128)(2,1)} all-to-all(bf16[8,16,10,2048]{3,1,2,0:T(8,128)(2,1)S(1)} %copy.35), channel_id=1, replica_groups=mesh['row'=2,'col'=4,'tok'=4] {'row','col'}, dimensions={0} | all-to-all | bytes 10485760 | tf_op jit(solution)/shard_map/all_to_all | solution.py:57
  175.9 421.0 %all-gather.3.cloned.1.call-done = bf16[16,2,768,2048]{3,2,1,0:T(8,128)(2,1)} async-done(((bf16[16,2,192,2048]{3,2,1,0:T(8,128)(2,1)}), bf16[16,2,768,2048]{3,2,1,0:T(8,128)(2,1)}) %all-gather.3.cloned.1.call-update) | async-done | bytes 100663312 | tf_op jit(solution)/shard_map/all_gather | solution.py:28
  596.9 58.9 %fusion.9 = f32[8,16,10,2,768]{4,2,3,0,1:T(8,128)} fusion(bf16[16,2,768,2048]{3,2,1,0:T(8,128)(2,1)} %all-gather.3.cloned.1.call-done, bf16[8,16,10,2048,1]{3,1,2,0,4:T(8,128)(2,1)} %bitcast.54), kind=kOutput, calls=%fused_computation.14 | convolution fusion | flops 8053063680 | bytes 113770496 | tf_op jit(solution)/shard_map/sjcd,jgfd->sjcgf/dot_general | solution.py:25
  655.8 241.6 %all-gather.5.cloned.1.call-done = bf16[16,768,2048]{2,1,0:T(8,128)(2,1)} async-done(((bf16[16,192,2048]{2,1,0:T(8,128)(2,1)}), bf16[16,768,2048]{2,1,0:T(8,128)(2,1)}) %all-gather.5.cloned.1.call-update) | async-done | bytes 50331664 | tf_op jit(solution)/shard_map/all_gather | solution.py:35
  897.5 24.4 %convert_bitcast_fusion = bf16[8,16,10,2048]{3,2,0,1:T(8,128)(2,1)} fusion(bf16[16,768,2048]{2,1,0:T(8,128)(2,1)} %all-gather.5.cloned.1.call-done, f32[8,16,10,2,768]{4,2,3,0,1:T(8,128)} %fusion.9), kind=kOutput, calls=%fused_computation.8 | convolution fusion | flops 4035051520 | bytes 63438848 | tf_op jit(solution)/shard_map/sjcf,jfd->sjcd/dot_general | solution.py:32
  921.9 9.1 copy.38
  931.0 5.6 all-to-all-start.1
  937.1 116.6 %all-to-all-done.1 = bf16[8,16,10,2048]{3,1,2,0:T(8,128)(2,1)} async-done(((bf16[8,16,10,2048]{3,1,2,0:T(8,128)(2,1)}), bf16[8,16,10,2048]{3,1,2,0:T(8,128)(2,1)}, u32[]{:S(2)}, u32[]{:S(2)}) %all-to-all-start.1) | async-done | bytes 5242912 | tf_op jit(solution)/shard_map/all_to_all | solution.py:59
  1053.6 9.7 copy.39
  1063.4 9.8 reshape.89
  1073.2 12.0 %gather_fusion.1 = bf16[1024,2048]{1,0:T(8,128)(2,1)} fusion(bf16[1280,2048]{1,0:T(8,128)(2,1)} %reshape.89, s32[1024]{0:T(1024)S(1)} %broadcast_clamp_fusion), kind=kCustom, calls=%fused_computation.1 | custom fusion | bytes 8392704 | tf_op jit(solution)/shard_map/jit(_take)/gather | solution.py:60
  1085.2 3.5 fusion.14
  1088.7 1.1 copy.53
  (47 shorter events, 1.7 us)
Async XLA Ops:
  6.5 590.4 %all-gather.3.cloned.1.call-start = ((), (), s32[]{:S(2)}) async-start(), calls=%async_computation.2 | async-start | bytes 125829120 | tf_op jit(solution)/shard_map/all_gather | solution.py:28
  7.3 0.8 copy-start.3
  7.3 7.1 copy-start
  7.3 7.3 copy-start.8
  7.3 890.2 %all-gather.5.cloned.1.call-start = ((), (), s32[]{:S(2)}) async-start(), calls=%async_computation.3 | async-start | bytes 62914560 | tf_op jit(solution)/shard_map/all_gather | solution.py:35
  9.4 0.6 copy-start.1
  10.0 4.3 copy-start.5
  930.9 5.6 copy-start.2
  930.9 5.8 copy-start.4
  930.9 5.9 copy-start.7
  930.9 6.1 copy-start.6
  931.0 122.7 %all-to-all-start.1 = ((bf16[8,16,10,2048]{3,1,2,0:T(8,128)(2,1)}), bf16[8,16,10,2048]{3,1,2,0:T(8,128)(2,1)}, u32[]{:S(2)}, u32[]{:S(2)}) async-start(bf16[8,16,10,2048]{3,1,2,0:T(8,128)(2,1)} %copy.38), calls=%async_computation.1 | async-start | bytes 10485760 | tf_op jit(solution)/shard_map/all_to_all | solution.py:59
Sparse Core Ops, SparseCore 0:
  8.9 587.9 all-gather.2
  598.5 298.9 all-gather.4
where the time goes:
time: 1100 us
  waiting for transfers between devices  781 us (71%)
  blocking collectives  123 us (11%)
  matrix products  86.8 us (8%)
  local copies, waits for them, and re-layouts  72.7 us (7%)
  other arithmetic  14 us (1%)
  between operations  13.6 us (1%)
    all_gather x1, waiting for transfers between devices, apply_experts(): lax.all_gather(gate_up_weight, 'tok', axis=2, tiled=True)  421 us
    all_gather x1, waiting for transfers between devices, apply_experts(): lax.all_gather(down_weight, 'tok', axis=1, tiled=True)  242 us
    all_to_all x1, blocking collectives, local(): lax.all_to_all(outbound, ('row', 'col'), split_axis=0, concat_axis=0, til...  123 us
    all_to_all x1, waiting for transfers between devices, local(): lax.all_to_all(results, ('row', 'col'), split_axis=0, concat_axis=0, tile...  117 us
    dot_general x1, matrix products, apply_experts(): jnp.einsum('sjcd,jgfd->sjcgf', received, lax.all_gather(gate_up_weight, '...  58.9 us
    dot_general x1, matrix products, apply_experts(): jnp.einsum('sjcf,jfd->sjcd', hidden, lax.all_gather(down_weight, 'tok', a...  24.4 us
  transfers between devices with their start and end apart: 3, of which 3 were waited for; matrix products, arithmetic and copies ran while one was open for 9% of the time, Pallas kernels for 0%

commit v1 on v0

--- a/solution.py
+++ b/solution.py
@@ -5,6 +5,22 @@
 
 CAP = 10
 EPSILON = 1e-06
+
+
+def product_in_turn(x, axis, dim, term):
+    count, index, width = (lax.axis_size(axis), lax.axis_index(axis), x.shape[dim])
+    upward = [(i, (i + 1) % count) for i in range(count)]
+    behind = [(i, (i - 1) % count) for i in range(count)]
+    middle = count // 2
+    from_left = from_right = x
+    total = term(x, index * width)
+    for step in range(1, middle + 1):
+        from_left = lax.ppermute(from_left, axis, upward)
+        if step < count - middle:
+            from_right = lax.ppermute(from_right, axis, behind)
+            total = total + term(from_right, (index + step) % count * width)
+        total = total + term(from_left, (index - step) % count * width)
+    return total
 
 
 def rank_in_block(block_routes, experts):
@@ -29,11 +45,16 @@
         preferred_element_type=jnp.float32,
     )
     hidden = (jax.nn.silu(both[:, :, :, 0, :]) * both[:, :, :, 1, :]).astype(jnp.bfloat16)
-    summed = jnp.einsum(
-        "sjcf,jfd->sjcd",
-        hidden,
-        lax.all_gather(down_weight, "tok", axis=1, tiled=True),
-        preferred_element_type=jnp.float32,
+    summed = product_in_turn(
+        down_weight,
+        "tok",
+        1,
+        lambda shard, start: jnp.einsum(
+            "sjcf,jfd->sjcd",
+            lax.dynamic_slice_in_dim(hidden, start, shard.shape[1], axis=3),
+            shard,
+            preferred_element_type=jnp.float32,
+        ),
     )
     return summed.astype(jnp.bfloat16)
 

time: 1100 us -> 1250 us (1.14)
  waiting for transfers between devices: 781 us -> 1010 us
  blocking collectives: 123 us -> 0 us
  matrix products: 86.8 us -> 113 us
  starting transfers between devices: 5.67 us -> 20.6 us
    ppermute x0 -> x3, waiting for transfers between devices: none -> 360 us  [the longest x2 360 us: product_in_turn(): from_left = lax.ppermute(from_left, axis, upward)]
    all_gather x1 -> x0, waiting for transfers between devices: 242 us -> none  [apply_experts(): lax.all_gather(down_weight, 'tok', axis=1, tiled=True)]
    all_to_all x1 -> x0, blocking collectives: 123 us -> none  [local(): lax.all_to_all(outbound, ('row', 'col'), split_axis=0, concat_axis=0, til...]
    all_gather x1, waiting for transfers between devices: 421 us -> 531 us  [apply_experts(): lax.all_gather(gate_up_weight, 'tok', axis=2, tiled=True)]
    dot_general x1 -> x4, matrix products: 24.4 us -> 60.5 us  [apply_experts(): jnp.einsum('sjcf,jfd->sjcd', lax.dynamic_slice_in_dim(hidden, start, shar...]
  transfers between devices with their start and end apart: 3 -> 6, of which waited for: 3 -> 3; matrix products, arithmetic and copies ran while one was open for 9% -> 11% of each run, Pallas kernels for 0% -> 0%
where the time goes in v1:
time: 1250 us
  waiting for transfers between devices  1010 us (81%)
  matrix products  113 us (9%)
  local copies, waits for them, and re-layouts  72.7 us (6%)
  starting transfers between devices  20.6 us (2%)
  other arithmetic  20 us (2%)
  between operations  13.6 us (1%)
    all_gather x1, waiting for transfers between devices, apply_experts(): lax.all_gather(gate_up_weight, 'tok', axis=2, tiled=True)  531 us
    ppermute x2, waiting for transfers between devices, product_in_turn(): from_left = lax.ppermute(from_left, axis, upward)  360 us
    all_to_all x1, waiting for transfers between devices, local(): lax.all_to_all(results, ('row', 'col'), split_axis=0, concat_axis=0, tile...  116 us
    dot_general x4, matrix products, apply_experts(): jnp.einsum('sjcf,jfd->sjcd', lax.dynamic_slice_in_dim(hidden, start, shar...  60.5 us
    dot_general x1, matrix products, apply_experts(): jnp.einsum('sjcd,jgfd->sjcgf', received, lax.all_gather(gate_up_weight, '...  48.9 us
  transfers between devices with their start and end apart: 6, of which 3 were waited for; matrix products, arithmetic and copies ran while one was open for 11% of the time, Pallas kernels for 0%

profile of v1, /device:TPU:0, one launch (start us, length us, event | category | flops | bytes accessed | tf_op | source)
XLA Modules:
  0.0 1248.1 jit_solution(1133546867489938162)
XLA Ops:
  9.7 4.3 scatter_custom_fusion
  14.5 6.1 gather_fusion
  20.6 10.5 gather.13
  31.3 13.0 %broadcast_select_fusion = bf16[8,16,10,2048]{3,2,1,0:T(8,128)(2,1)} fusion(bf16[8,16,10,2048]{3,2,1,0:T(8,128)(2,1)} %gather.13, pred[8,16,10]{2,1,0:T(8,128)(4,1)S(1)} %broadcast_in_dim.34), kind=kLoop, calls=%fused_computation.16 | loop fusion | flops 2621440 | bytes 10487040 | tf_op jit(solution)/shard_map/jit(_take)/select_n | solution.py:76
  44.3 12.0 copy.35
  56.3 6.3 all-to-all-start
  62.6 1.3 collective-permute-start
  63.9 360.0 %collective-permute-done.1 = bf16[16,192,2048]{2,1,0:T(8,128)(2,1)} collective-permute-done((bf16[16,192,2048]{2,1,0:T(8,128)(2,1)}, bf16[16,192,2048]{2,1,0:T(8,128)(2,1)}, u32[]{:S(2)}, u32[]{:S(2)}) %collective-permute-start.1) | collective-permute-done | bytes 12582944 | tf_op jit(solution)/shard_map/ppermute | solution.py:18
  423.9 5.7 collective-permute-start.2
  429.6 531.3 %all-gather.2.cloned.1.call-done = bf16[16,2,768,2048]{3,2,1,0:T(8,128)(2,1)} async-done(((bf16[16,2,192,2048]{3,2,1,0:T(8,128)(2,1)}), bf16[16,2,768,2048]{3,2,1,0:T(8,128)(2,1)}) %all-gather.2.cloned.1.call-update) | async-done | bytes 100663312 | tf_op jit(solution)/shard_map/all_gather | solution.py:44
  960.9 48.9 %fusion.14 = f32[8,16,10,2,768]{4,2,3,0,1:T(8,128)} fusion(bf16[16,2,768,2048]{3,2,1,0:T(8,128)(2,1)} %all-gather.2.cloned.1.call-done, bf16[8,16,10,2048,1]{3,1,2,0,4:T(8,128)(2,1)} %bitcast.6), kind=kOutput, calls=%fused_computation.21 | convolution fusion | flops 8053063680 | bytes 113770496 | tf_op jit(solution)/shard_map/sjcd,jgfd->sjcgf/dot_general | solution.py:41
  1009.8 5.9 fusion.13
  1015.7 13.9 %fusion.8 = f32[16,8,10,2048]{3,2,1,0:T(8,128)} fusion(bf16[16,192,2048]{2,1,0:T(8,128)(2,1)} %param.11, bf16[8,16,10,768]{3,2,0,1:T(8,128)(2,1)S(1)} %fusion.13, s32[]{:T(128)S(6)} %select_n.69), kind=kOutput, calls=%fused_computation.12 | convolution fusion | flops 1006632960 | bytes 24117252 | tf_op jit(solution)/shard_map/sjcf,jfd->sjcd/dot_general | solution.py:52
  1029.5 12.7 %fusion.4 = f32[16,8,10,2048]{3,2,1,0:T(8,128)} fusion(bf16[16,192,2048]{2,1,0:T(8,128)(2,1)} %collective-permute-done.1, bf16[8,16,10,768]{3,2,0,1:T(8,128)(2,1)S(1)} %fusion.13, s32[]{:T(128)S(6)} %select_n.73), kind=kOutput, calls=%fused_computation.8 | convolution fusion | flops 1006632960 | bytes 24117252 | tf_op jit(solution)/shard_map/sjcf,jfd->sjcd/dot_general | solution.py:52
  1042.2 12.7 %fusion.6 = f32[16,8,10,2048]{3,2,1,0:T(8,128)} fusion(bf16[16,192,2048]{2,1,0:T(8,128)(2,1)} %collective-permute-done, bf16[8,16,10,768]{3,2,0,1:T(8,128)(2,1)S(1)} %fusion.13, s32[]{:T(128)S(6)} %select_n.71), kind=kOutput, calls=%fused_computation.10 | convolution fusion | flops 1006632960 | bytes 24117252 | tf_op jit(solution)/shard_map/sjcf,jfd->sjcd/dot_general | solution.py:52
  1055.0 21.2 %fusion.10 = bf16[8,16,10,2048]{3,2,0,1:T(8,128)(2,1)S(1)} fusion(f32[16,8,10,2048]{3,2,1,0:T(8,128)} %fusion.4, f32[16,8,10,2048]{3,2,1,0:T(8,128)} %fusion.8, f32[16,8,10,2048]{3,2,1,0:T(8,128)} %fusion.6, bf16[16,192,2048]{2,1,0:T(8,128)(2,1)} %collective-permute-done.2, bf16[8,16,10,768]{3,2,0,1:T(8,128)(2,1)} %copy-done, s32[]{:T(128)S(6)} %select_n.75), kind=kOutput, calls=%fused_computation.14 | convolution fusion | flops 1017118720 | bytes 69206016 | tf_op jit(solution)/shard_map/sjcf,jfd->sjcd/dot_general | solution.py:52
  1076.1 5.3 copy.38
  1081.5 6.7 all-to-all-start.1
  1088.7 116.4 %all-to-all-done.1 = bf16[8,16,10,2048]{3,1,2,0:T(8,128)(2,1)} async-done(((bf16[8,16,10,2048]{3,1,2,0:T(8,128)(2,1)}), bf16[8,16,10,2048]{3,1,2,0:T(8,128)(2,1)}, u32[]{:S(2)}, u32[]{:S(2)}) %all-to-all-start.1) | async-done | bytes 5242912 | tf_op jit(solution)/shard_map/all_to_all | solution.py:80
  1205.2 9.7 copy.39
  1214.9 9.8 reshape.89
  1224.7 12.0 gather_fusion.1
  1236.7 3.5 fusion.19
  1240.2 1.1 copy.56
  (57 shorter events, 4.2 us)
Async XLA Ops:
  6.5 1.2 copy-start.4
  6.5 7.6 copy-start.1
  6.5 7.8 copy-start.9
  6.5 954.3 %all-gather.2.cloned.1.call-start = ((), (), s32[]{:S(2)}) async-start(), calls=%async_computation.2 | async-start | bytes 125829120 | tf_op jit(solution)/shard_map/all_gather | solution.py:44
  7.3 416.6 %collective-permute-start.1 = (bf16[16,192,2048]{2,1,0:T(8,128)(2,1)}, bf16[16,192,2048]{2,1,0:T(8,128)(2,1)}, u32[]{:S(2)}, u32[]{:S(2)}) collective-permute-start(bf16[16,192,2048]{2,1,0:T(8,128)(2,1)} %param.11), channel_id=1, source_target_pairs={{0,1},{1,2},{2,3},{3,0},{4,5},{5,6},{6,7},{7,4},{8,9},{9,10},{10,1... | collective-permute-start | bytes 37748744 | tf_op jit(solution)/shard_map/ppermute | solution.py:18
  9.1 0.6 copy-start.2
  9.7 4.3 copy-start.6
  56.3 373.3 %all-to-all-start = ((bf16[8,16,10,2048]{3,1,2,0:T(8,128)(2,1)}), bf16[8,16,10,2048]{3,1,2,0:T(8,128)(2,1)}, u32[]{:S(2)}, u32[]{:S(2)}) async-start(bf16[8,16,10,2048]{3,1,2,0:T(8,128)(2,1)} %copy.35), calls=%async_computation | async-start | bytes 10485760 | tf_op jit(solution)/shard_map/all_to_all | solution.py:78
  62.6 979.6 %collective-permute-start = (bf16[16,192,2048]{2,1,0:T(8,128)(2,1)}, bf16[16,192,2048]{2,1,0:T(8,128)(2,1)}, u32[]{:S(2)}, u32[]{:S(2)}) collective-permute-start(bf16[16,192,2048]{2,1,0:T(8,128)(2,1)} %param.11), channel_id=1, source_target_pairs={{0,3},{1,0},{2,1},{3,2},{4,7},{5,4},{6,5},{7,6},{8,11},{9,8},{10,9... | collective-permute-start | bytes 37748744 | tf_op jit(solution)/shard_map/ppermute | solution.py:20
  423.9 631.1 %collective-permute-start.2 = (bf16[16,192,2048]{2,1,0:T(8,128)(2,1)}, bf16[16,192,2048]{2,1,0:T(8,128)(2,1)}, u32[]{:S(2)}, u32[]{:S(2)}) collective-permute-start(bf16[16,192,2048]{2,1,0:T(8,128)(2,1)} %collective-permute-done.1), channel_id=1, source_target_pairs={{0,1},{1,2},{2,3},{3,0},{4,5},{5,6},{6,7},{7,4},{8,9},{9,10},{10,1... | collective-permute-start | bytes 37748744 | tf_op jit(solution)/shard_map/ppermute | solution.py:18
  1015.7 26.6 %copy-start = (bf16[8,16,10,768]{3,2,0,1:T(8,128)(2,1)}, bf16[8,16,10,768]{3,2,0,1:T(8,128)(2,1)S(1)}, u32[]{:S(2)}) copy-start(bf16[8,16,10,768]{3,2,0,1:T(8,128)(2,1)S(1)} %fusion.13) | copy-start | bytes 5898244
  1081.5 6.7 copy-start.3
  1081.5 6.9 copy-start.5
  1081.5 7.0 copy-start.8
  1081.5 7.2 copy-start.7
  1081.5 123.7 %all-to-all-start.1 = ((bf16[8,16,10,2048]{3,1,2,0:T(8,128)(2,1)}), bf16[8,16,10,2048]{3,1,2,0:T(8,128)(2,1)}, u32[]{:S(2)}, u32[]{:S(2)}) async-start(bf16[8,16,10,2048]{3,1,2,0:T(8,128)(2,1)} %copy.38), calls=%async_computation.1 | async-start | bytes 10485760 | tf_op jit(solution)/shard_map/all_to_all | solution.py:80
Sparse Core Ops, SparseCore 0:
  8.9 951.8 all-gather.1
